TPU v7x, 128 devices: a whole 4x4x4 slice. The times are simulated.
128 devices in a mesh: grp: 2 (over core), fsdp: 64 (over x, y, z).
Axes of the slice: x: 4, y: 4, z: 4, core: 2. Of those that a mesh axis runs over, the one named last changes fastest.
Arguments:
- item_states: bfloat16 [512, 256, 2048], P(('grp', 'fsdp')), may hold values from -6 to 6
- w_query: bfloat16 [2048, 2048], P('fsdp'), may hold values from -0.125 to 0.125
- w_key: bfloat16 [2048, 256], P('fsdp'), may hold values from -0.125 to 0.125
- w_value: bfloat16 [2048, 256], P('fsdp'), may hold values from -0.125 to 0.125
- item_gain: float32 [2048], replicated, may hold values from 0.25 to 1.75
- w_adapt: bfloat16 [2048, 4096], P('fsdp'), may hold values from -0.125 to 0.125
- user_gain: float32 [4096], replicated, may hold values from 0.25 to 1.75
- user_query: bfloat16 [4096, 128], P('fsdp'), may hold values from -0.5 to 0.5
- hist_owner: int32 [128, 128, 1], P(('grp', 'fsdp')), may hold values from 0 to 127; in each aligned block of 128 rows (0 to 127, 128 to 255, ..., all dimensions but the last counted through in order) at most 2 rows name the same one
- history_position_index: int32 [128, 128], P(('grp', 'fsdp')), may hold values from 0 to 3
- cotangent: bfloat16 [128, 128, 4096], P(('grp', 'fsdp')), may hold values from -6 to 6
Outputs:
- item_embed: bfloat16 [512, 2048], P(('grp', 'fsdp'))
- user_attention_output: bfloat16 [128, 128, 4096], P(('grp', 'fsdp'))
- item_grad: float32 [512, 2048], P(('grp', 'fsdp'))
Inputs may be any that keep to these rules, and one draw needn't show every extreme that they name: `hist_owner`: within one history no device is named by more than 2 positions, and some device is named by exactly 2 positions.
All inputs are finite; a program needn't handle non-finite values.
Results may differ from a plain program's by a relative error of at most 0.011.
Values may be sent and summed in bfloat16 or wider, within the bound.
No kernel may reach another device: no remote copies, remote signals or barrier semaphores. Data moves between devices by JAX's collectives and lax.ppermute only.
A program may use at most 128 MiB of HBM per device.

v0:
```python
import jax
import jax.numpy as jnp
from jax import lax
from jax.sharding import PartitionSpec as P

DI = 2048
IHEADS = 32
IHD = 64
IKV = 4
UHEADS = 32
UHD = 128
ILEN = 256


def stored(values):
    return lax.optimization_barrier(values.astype(jnp.bfloat16))


def rms_scale(values, gain):
    mean_sq = jnp.mean(values * values, axis=-1, keepdims=True)
    return values * lax.rsqrt(mean_sq + 1e-05) * gain


def item_pool(states, key_rows, value_rows, query_rows, item_gain):
    count = states.shape[0]
    group = IHEADS // IKV
    query_heads = query_rows.reshape(count, IKV, group, IHD).astype(jnp.float32)
    key_heads = key_rows.reshape(count, ILEN, IKV, IHD).astype(jnp.float32)
    value_heads = value_rows.reshape(count, ILEN, IKV, IHD).astype(jnp.float32)
    scores = jnp.einsum("igrd,itgd->igrt", query_heads, key_heads) * IHD ** (-0.5)
    weights = stored(jax.nn.softmax(scores, axis=-1)).astype(jnp.float32)
    mixed = jnp.einsum("igrt,itgd->igrd", weights, value_heads).reshape(count, IHEADS * IHD)
    last_row = states[:, ILEN - 1, :].astype(jnp.float32)
    return rms_scale(last_row + mixed, item_gain).astype(jnp.bfloat16)


def user_layer(hidden, user_gain, user_query):
    length_total = hidden.shape[0]
    normed = stored(rms_scale(hidden.astype(jnp.float32), user_gain)).astype(jnp.float32)
    heads = normed.reshape(length_total, UHEADS, UHD)
    query_map = user_query.reshape(UHEADS, UHD, UHD).astype(jnp.float32)
    queries = stored(jnp.einsum("thd,hde->the", heads, query_map)).astype(jnp.float32)
    scores = jnp.einsum("the,she->hts", queries, heads) * UHD ** (-0.5)
    target = jnp.arange(length_total, dtype=jnp.int32)
    causal = target[None, :, None] >= target[None, None, :]
    scores = jnp.where(causal, scores, -1e30)
    weights = stored(jax.nn.softmax(scores, axis=-1)).astype(jnp.float32)
    mixed = jnp.einsum("hts,shd->thd", weights, heads).reshape(length_total, UHEADS * UHD)
    return (hidden.astype(jnp.float32) + mixed).astype(jnp.bfloat16)


def serve_rows(requests, lookup_matrix):
    chosen_items = (
        requests[..., None] == jnp.arange(lookup_matrix.shape[0], dtype=jnp.int32)
    ).astype(lookup_matrix.dtype)
    return jnp.einsum(
        "ltj,jy->lty", chosen_items, lookup_matrix, preferred_element_type=jnp.float32
    ).astype(lookup_matrix.dtype)


def per_device(
    item_states,
    w_query,
    w_key,
    w_value,
    item_gain,
    w_adapt,
    user_gain,
    user_query,
    hist_owner,
    history_position_index,
    cotangent,
):
    groups = lax.axis_size("grp")
    shards = lax.axis_size("fsdp")
    devices = groups * shards
    count = item_states.shape[0]
    flat = item_states.reshape(count * ILEN, DI)
    last_row = item_states[:, ILEN - 1, :]
    packed = jnp.concatenate(
        [w_key, w_value, w_query, w_adapt, user_query.reshape(w_key.shape[0], -1)], axis=1
    )
    gathered = lax.all_gather(packed, "fsdp", axis=0, tiled=True)
    kv_cols = w_key.shape[1] + w_value.shape[1]
    q_end = kv_cols + w_query.shape[1]
    a_end = q_end + w_adapt.shape[1]
    kv_sum = jnp.dot(flat, gathered[:, :kv_cols], preferred_element_type=jnp.float32)
    key_sum = kv_sum[:, : w_key.shape[1]]
    summed_value = kv_sum[:, w_key.shape[1] :]
    query_sum = jnp.dot(last_row, gathered[:, kv_cols:q_end], preferred_element_type=jnp.float32)
    adapter = gathered[:, q_end:a_end]
    query_map = gathered[:, a_end:].reshape(-1, user_query.shape[1])
    item_embed = item_pool(
        item_states, stored(key_sum), stored(summed_value), stored(query_sum), item_gain
    )
    length_total = history_position_index.shape[1]
    cap_slots = max(2, 2 * length_total // devices)
    owner_users = hist_owner[0, :, 0]
    owner_hot = (owner_users[:, None] == jnp.arange(devices, dtype=jnp.int32)[None, :]).astype(
        jnp.int32
    )
    earlier = jnp.cumsum(owner_hot, axis=0) - owner_hot
    rank_in = jnp.sum(owner_hot * earlier, axis=1)
    position = owner_users * cap_slots + rank_in
    request = (
        jnp.full((devices * cap_slots,), count, jnp.int32)
        .at[position]
        .set(history_position_index[0])
    )
    request = request.reshape(devices, cap_slots)
    width = item_embed.shape[1]
    incoming = lax.all_to_all(request, ("grp", "fsdp"), split_axis=0, concat_axis=0, tiled=True)
    found = serve_rows(incoming, item_embed)
    returned = lax.all_to_all(found, ("grp", "fsdp"), split_axis=0, concat_axis=0, tiled=True)
    fetched = jnp.take(returned.reshape(devices * cap_slots, width), position, axis=0)
    hidden = stored(jnp.dot(fetched, adapter, preferred_element_type=jnp.float32))
    user_attention_output, pull = jax.vjp(
        lambda values: user_layer(values, user_gain, query_map), hidden
    )
    (grad_hidden,) = pull(cotangent[0])
    grad_rows = jnp.dot(grad_hidden, adapter.T, preferred_element_type=jnp.float32)
    outgoing = jnp.zeros((devices * cap_slots, DI), jnp.float32).at[position].set(grad_rows)
    arrived = lax.all_to_all(
        outgoing.reshape(devices, cap_slots, DI).astype(jnp.bfloat16),
        ("grp", "fsdp"),
        split_axis=0,
        concat_axis=0,
        tiled=True,
    ).astype(jnp.float32)
    terms = arrived.reshape(devices * cap_slots, DI)
    slot_hot = (
        incoming.reshape(-1)[:, None] == jnp.arange(count, dtype=jnp.int32)[None, :]
    ).astype(jnp.float32)
    item_grad = jnp.dot(slot_hot.T, terms, precision=lax.Precision.HIGHEST)
    return (item_embed, user_attention_output[None], item_grad)


def solution(mesh):
    placed = (
        P(("grp", "fsdp"), None, None),
        P("fsdp", None),
        P("fsdp", None),
        P("fsdp", None),
        P(),
        P("fsdp", None),
        P(),
        P("fsdp", None),
        P(("grp", "fsdp"), None, None),
        P(("grp", "fsdp"), None),
        P(("grp", "fsdp"), None, None),
    )
    return jax.shard_map(
        per_device,
        mesh=mesh,
        in_specs=placed,
        out_specs=(
            P(("grp", "fsdp"), None),
            P(("grp", "fsdp"), None, None),
            P(("grp", "fsdp"), None),
        ),
        check_vma=False,
    )
```

profile of v0, /device:TPU:1, one launch (start us, length us, event | category | flops | bytes accessed | tf_op | source)
XLA Modules:
  0.0 279.0 jit_solution(11355290367567312266)
XLA Ops:
  7.2 0.7 constant_dynamic-update-slice_fusion.4
  7.9 0.7 reshape.146
  8.7 0.7 constant_dynamic-update-slice_fusion.3
  9.4 0.9 constant_dynamic-update-slice_fusion.2
  10.3 1.0 constant_dynamic-update-slice_fusion.1
  11.3 0.8 copy-done.9
  12.1 0.7 fusion.76
  12.8 0.2 reduce_window_sum.11
  13.0 0.8 select_reduce_fusion
  13.8 0.7 fusion.80
  14.5 1.1 scatter_custom_fusion
  15.6 0.8 all_to_all.12
  16.4 11.5 %all-to-all-start = ((s32[128,1,2]{2,1,0:T(1,128)}), s32[128,1,2]{2,1,0:T(1,128)S(1)}, u32[]{:S(2)}, u32[]{:S(2)}) async-start(s32[128,1,2]{2,1,0:T(1,128)} %bitcast.9), calls=%async_computation | async-start | bytes 131072 | tf_op jit(solution)/shard_map/all_to_all | solution.py:112
  27.9 0.9 slice.24
  28.8 0.1 reshape.157
  28.9 8.5 %all-to-all-done = s32[128,1,2]{2,1,0:T(1,128)S(1)} async-done(((s32[128,1,2]{2,1,0:T(1,128)}), s32[128,1,2]{2,1,0:T(1,128)S(1)}, u32[]{:S(2)}, u32[]{:S(2)}) %all-to-all-start) | async-done | bytes 1056 | tf_op jit(solution)/shard_map/all_to_all | solution.py:112
  37.5 120.2 %all-gather.2.cloned.1.call-done = bf16[2048,6912]{1,0:T(8,128)(2,1)} async-done(((bf16[32,6912]{1,0:T(8,128)(2,1)}), bf16[2048,6912]{1,0:T(8,128)(2,1)}) %all-gather.2.cloned.1.call-update) | async-done | bytes 28311568 | tf_op jit(solution)/shard_map/all_gather | solution.py:83
  157.8 4.6 %fusion.14 = bf16[4,2048]{1,0:T(4,128)(2,1)S(1)} fusion(bf16[2048,6912]{1,0:T(8,128)(2,1)} %all-gather.2.cloned.1.call-done, bf16[4,1,2048]{2,1,0:T(2,128)(2,1)S(1)} %slice.24), kind=kOutput, calls=%fused_computation.22 | convolution fusion | flops 33562624 | bytes 8421376 | tf_op jit(solution)/shard_map/dot_general | solution.py:90
  162.3 0.1 reshape.147
  162.4 5.2 %fusion.35 = bf16[1024,512]{0,1:T(8,128)(2,1)S(1)} fusion(bf16[1024,2048]{1,0:T(8,128)(2,1)} %bitcast.113, bf16[2048,6912]{1,0:T(8,128)(2,1)} %all-gather.2.cloned.1.call-done), kind=kOutput, calls=%fused_computation.47 | convolution fusion | flops 2148007936 | bytes 7340032 | tf_op jit(solution)/shard_map/dot_general | solution.py:87
  167.8 0.4 reshape.149
  168.1 0.3 fusion.98
  168.5 0.1 divide_convert_fusion.1
  168.6 0.4 reshape.150
  169.0 0.3 multiply_reduce_fusion
  169.3 0.1 reshape.151
  169.5 0.5 convolution_convert_fusion
  170.0 2.0 copy.51
  172.1 8.5 %all-to-all-start.1 = ((bf16[128,2,2048]{2,1,0:T(2,128)(2,1)}), bf16[128,2,2048]{2,1,0:T(2,128)(2,1)}, u32[]{:S(2)}, u32[]{:S(2)}) async-start(bf16[128,2,2048]{2,1,0:T(2,128)(2,1)} %copy.51), calls=%async_computation.1 | async-start | bytes 2097152 | tf_op jit(solution)/shard_map/all_to_all | solution.py:114
  180.6 0.7 copy.75
  181.3 0.5 slice-done
  181.8 0.4 reshape_reshape.3
  182.2 15.8 %all-to-all-done.1 = bf16[128,2,2048]{2,1,0:T(2,128)(2,1)} async-done(((bf16[128,2,2048]{2,1,0:T(2,128)(2,1)}), bf16[128,2,2048]{2,1,0:T(2,128)(2,1)}, u32[]{:S(2)}, u32[]{:S(2)}) %all-to-all-start.1) | async-done | bytes 1048608 | tf_op jit(solution)/shard_map/all_to_all | solution.py:114
  198.1 1.5 reshape.152
  199.5 1.7 gather_fusion
  201.3 8.4 %fusion.8 = bf16[128,4096]{1,0:T(8,128)(2,1)S(1)} fusion(bf16[2048,6912]{1,0:T(8,128)(2,1)} %all-gather.2.cloned.1.call-done, bf16[128,2048]{1,0:T(8,128)(2,1)} %gather_fusion, pred[128]{0:T(512)(128)(4,1)S(1)} %compare_and_fusion), kind=kOutput, calls=%fused_computation.11 | convolution fusion | flops 2148270080 | bytes 18350208 | tf_op jit(solution)/shard_map/dot_general | solution.py:116
  209.6 0.3 fusion.24
  210.0 0.3 fusion.26
  210.3 1.9 fusion.38
  212.1 1.4 fusion.39
  213.6 3.5 %fusion.99 = (f32[32,128]{1,0:T(8,128)S(1)}, f32[32,128,128]{1,2,0:T(8,128)}) fusion(pred[128,128]{0,1:T(8,128)(4,1)S(1)} %iota_compare_fusion.2, bf16[128,32,128]{0,2,1:T(8,128)(2,1)} %fusion.38, bf16[128,4096]{1,0:T(8,128)(2,1)S(1)} %fusion.26), kind=kOutput, calls=%fused_computation.124 | convolution fusion | flops 136315008 | bytes 4227072 | tf_op jit(solution)/shard_map/jvp()/sub | solution.py:47
  217.1 2.6 fusion.22
  219.7 0.2 copy-done.5
  219.9 0.3 copy-done.6
  220.2 0.9 fusion.95
  221.0 0.8 fusion.40
  221.8 0.9 fusion.104
  222.7 2.0 fusion.51
  224.6 0.9 add_convert_fusion
  225.5 1.3 copy.76
  226.8 0.6 copy-done.2
  227.5 1.9 copy.74
  229.4 3.5 %fusion.28 = (f32[128]{0:T(128)S(1)}, bf16[1,128,4096]{2,1,0:T(8,128)(2,1)}) fusion(bf16[128,4096]{1,0:T(8,128)(2,1)S(1)} %copy-done.1, bf16[128,4096]{1,0:T(8,128)(2,1)} %copy.76, f32[4096]{0:T(1024)S(1)} %copy-done.10, f32[128,4096]{1,0:T(8,128)} %copy.74), kind=kLoop, calls=%fused_computation.34 | loop fusion | flops 3669888 | bytes 5259776 | tf_op jit(solution)/shard_map/transpose(jvp())/reduce_sum | solution.py:21
  232.9 10.4 %fusion.2 = f32[128,2048]{1,0:T(8,128)} fusion(bf16[2048,6912]{1,0:T(8,128)(2,1)} %all-gather.2.cloned.1.call-done, bf16[128,4096]{1,0:T(8,128)(2,1)S(1)} %copy-done.1, bf16[128,4096]{1,0:T(8,128)(2,1)S(1)} %copy-done.4, bf16[1,128,4096]{2,1,0:T(8,128)(2,1)S(1)} %copy-done.8, f32[128]{0:T(128)S(1)} %multiply_multiply_fusion, f32[4096]{0:T(1024)S(1)} %copy-done.10, ...), kind=kOutput, calls=%fused_computation.5 | convolution fusion | flops 2152202240 | bytes 20988928 | tf_op jit(solution)/shard_map/dot_general | solution.py:121
  243.3 2.4 scatter_custom_fusion.1
  245.7 0.1 convert_element_type.127
  245.9 1.5 convert_element_type.128
  247.4 5.5 %all-to-all-start.2 = ((bf16[128,2,2048]{2,1,0:T(2,128)(2,1)}), bf16[128,2,2048]{2,1,0:T(2,128)(2,1)S(1)}, u32[]{:S(2)}, u32[]{:S(2)}) async-start(bf16[128,2,2048]{2,1,0:T(2,128)(2,1)} %convert_element_type.128), calls=%async_computation.2 | async-start | bytes 2097152 | tf_op jit(solution)/shard_map/all_to_all | solution.py:123
  252.9 0.5 broadcast.136
  253.4 0.8 reduce.4
  254.2 0.1 eq.50
  254.4 16.4 %all-to-all-done.2 = bf16[128,2,2048]{2,1,0:T(2,128)(2,1)S(1)} async-done(((bf16[128,2,2048]{2,1,0:T(2,128)(2,1)}), bf16[128,2,2048]{2,1,0:T(2,128)(2,1)S(1)}, u32[]{:S(2)}, u32[]{:S(2)}) %all-to-all-start.2) | async-done | bytes 1048608 | tf_op jit(solution)/shard_map/all_to_all | solution.py:123
  270.7 0.4 reshape.156
  271.2 1.0 fusion.74
  (40 shorter events, 0.4 us)
Async XLA Ops:
  7.2 150.6 %all-gather.2.cloned.1.call-start = ((), (), s32[]{:S(2)}) async-start(), calls=%async_computation.3 | async-start | bytes 28753920 | tf_op jit(solution)/shard_map/all_gather | solution.py:83
  11.3 0.8 copy-start.9
  16.4 21.1 %all-to-all-start = ((s32[128,1,2]{2,1,0:T(1,128)}), s32[128,1,2]{2,1,0:T(1,128)S(1)}, u32[]{:S(2)}, u32[]{:S(2)}) async-start(s32[128,1,2]{2,1,0:T(1,128)} %bitcast.9), calls=%async_computation | async-start | bytes 131072 | tf_op jit(solution)/shard_map/all_to_all | solution.py:112
  167.7 1.7 copy-start.12
  169.5 2.6 copy-start.11
  170.0 10.6 %copy-start.7 = (bf16[1,128,4096]{2,1,0:T(8,128)(2,1)S(1)}, bf16[1,128,4096]{2,1,0:T(8,128)(2,1)}, u32[]{:S(2)}) copy-start(bf16[1,128,4096]{2,1,0:T(8,128)(2,1)} %param.21) | copy-start | bytes 3145732
  172.1 9.2 %copy-start.13 = (s32[1,128,1]{1,2,0:T(1,128)S(1)}, s32[1,128,1]{1,2,0:T(1,128)}, u32[]{:S(2)}) copy-start(s32[1,128,1]{1,2,0:T(1,128)} %param.19) | copy-start | bytes 1540
  172.1 26.0 %all-to-all-start.1 = ((bf16[128,2,2048]{2,1,0:T(2,128)(2,1)}), bf16[128,2,2048]{2,1,0:T(2,128)(2,1)}, u32[]{:S(2)}, u32[]{:S(2)}) async-start(bf16[128,2,2048]{2,1,0:T(2,128)(2,1)} %copy.51), calls=%async_computation.1 | async-start | bytes 2097152 | tf_op jit(solution)/shard_map/all_to_all | solution.py:114
  180.6 1.2 slice-start
  201.3 8.7 %copy-start.10 = (f32[4096]{0:T(1024)S(1)}, f32[4096]{0:T(1024)}, u32[]{:S(2)}) copy-start(f32[4096]{0:T(1024)} %param.17) | copy-start | bytes 49156
  209.6 2.5 copy-start
  217.0 2.6 copy-start.3
  217.0 2.9 %copy-start.5 = (f32[32,128,128]{1,2,0:T(8,128)S(1)}, f32[32,128,128]{1,2,0:T(8,128)}, u32[]{:S(2)}) copy-start(f32[32,128,128]{1,2,0:T(8,128)} %get-tuple-element.14) | copy-start | bytes 6291460
  217.0 3.1 %copy-start.6 = (bf16[128,32,128]{0,2,1:T(8,128)(2,1)S(1)}, bf16[128,32,128]{0,2,1:T(8,128)(2,1)}, u32[]{:S(2)}) copy-start(bf16[128,32,128]{0,2,1:T(8,128)(2,1)} %fusion.38) | copy-start | bytes 3145732
  225.5 2.0 copy-start.2
  227.5 1.9 copy-start.1
  229.4 3.5 %copy-start.4 = (bf16[128,4096]{1,0:T(8,128)(2,1)S(1)}, bf16[128,4096]{1,0:T(8,128)(2,1)}, u32[]{:S(2)}) copy-start(bf16[128,4096]{1,0:T(8,128)(2,1)} %copy.76) | copy-start | bytes 3145732
  229.4 3.5 %copy-start.8 = (bf16[1,128,4096]{2,1,0:T(8,128)(2,1)S(1)}, bf16[1,128,4096]{2,1,0:T(8,128)(2,1)}, u32[]{:S(2)}) copy-start(bf16[1,128,4096]{2,1,0:T(8,128)(2,1)} %param.21) | copy-start | bytes 3145732
  247.4 23.3 %all-to-all-start.2 = ((bf16[128,2,2048]{2,1,0:T(2,128)(2,1)}), bf16[128,2,2048]{2,1,0:T(2,128)(2,1)S(1)}, u32[]{:S(2)}, u32[]{:S(2)}) async-start(bf16[128,2,2048]{2,1,0:T(2,128)(2,1)} %convert_element_type.128), calls=%async_computation.2 | async-start | bytes 2097152 | tf_op jit(solution)/shard_map/all_to_all | solution.py:123
Sparse Core Ops, SparseCore 0:
  12.2 145.5 all-gather.1
where the time goes:
time: 280 us; the launch traced here: 279 us
  waiting for transfers between devices  161 us (58%)
  matrix products  42.8 us (15%)
  starting transfers between devices  25.5 us (9%)
  local copies, waits for them, and re-layouts  25 us (9%)
  between operations  14.4 us (5%)
  other arithmetic  10.3 us (4%)
    all_gather x1, waiting for transfers between devices, per_device(): gathered = lax.all_gather(packed, 'fsdp', axis=0, tiled=True)  120 us
    all_to_all x1, waiting for transfers between devices, per_device(): lax.all_to_all(outgoing.reshape(devices, cap_slots, DI).astype(jnp.bfloat...  16.4 us
    all_to_all x1, waiting for transfers between devices, per_device(): lax.all_to_all(found, ('grp', 'fsdp'), split_axis=0, concat_axis=0, tiled...  15.8 us
    all_to_all x1, starting transfers between devices, per_device(): lax.all_to_all(request, ('grp', 'fsdp'), split_axis=0, concat_axis=0, til...  11.5 us
    dot_general x1, matrix products, per_device(): jnp.dot(grad_hidden, adapter.T, preferred_element_type=jnp.float32)  10.4 us
    all_to_all x1, waiting for transfers between devices, per_device(): lax.all_to_all(request, ('grp', 'fsdp'), split_axis=0, concat_axis=0, til...  8.54 us
    all_to_all x1, starting transfers between devices, per_device(): lax.all_to_all(found, ('grp', 'fsdp'), split_axis=0, concat_axis=0, tiled...  8.49 us
    dot_general x1, matrix products, per_device(): jnp.dot(fetched, adapter, preferred_element_type=jnp.float32)  8.37 us
  transfers between devices with their start and end apart: 4, of which 4 were waited for; matrix products, arithmetic and copies ran while one was open for 3% of the time, Pallas kernels for 0%

commit v1 on v0

--- a/solution.py
+++ b/solution.py
@@ -10,6 +10,11 @@
 UHEADS = 32
 UHD = 128
 ILEN = 256
+
+
+def gather_from_all(x, axis, dim):
+    copies = jnp.concatenate([x] * lax.axis_size(axis), axis=dim)
+    return lax.all_to_all(copies, axis, dim, dim, tiled=True)
 
 
 def stored(values):
@@ -80,7 +85,7 @@
     packed = jnp.concatenate(
         [w_key, w_value, w_query, w_adapt, user_query.reshape(w_key.shape[0], -1)], axis=1
     )
-    gathered = lax.all_gather(packed, "fsdp", axis=0, tiled=True)
+    gathered = gather_from_all(packed, "fsdp", 0)
     kv_cols = w_key.shape[1] + w_value.shape[1]
     q_end = kv_cols + w_query.shape[1]
     a_end = q_end + w_adapt.shape[1]

time: 280 us -> 1010 us (3.61); the launches traced: 279 us -> 998 us
  waiting for transfers between devices: 161 us -> 502 us
  local copies, waits for them, and re-layouts: 25 us -> 332 us
  starting transfers between devices: 25.5 us -> 103 us
  between operations: 14.4 us -> 1.17 us
    all_to_all x0 -> x1, waiting for transfers between devices: none -> 472 us  [gather_from_all(): return lax.all_to_all(copies, axis, dim, dim, tiled=True)]
    unnamed x32 -> x337, local copies, waits for them, and re-layouts: 5.25 us -> 310 us
    all_gather x1 -> x0, waiting for transfers between devices: 120 us -> none  [per_device(): gathered = lax.all_gather(packed, 'fsdp', axis=0, tiled=True)]
    all_to_all x1, starting transfers between devices: 8.49 us -> 74.9 us  [per_device(): lax.all_to_all(found, ('grp', 'fsdp'), split_axis=0, concat_axis=0, tiled...]
    all_to_all x0 -> x1, starting transfers between devices: none -> 10.9 us  [gather_from_all(): return lax.all_to_all(copies, axis, dim, dim, tiled=True)]
  transfers between devices with their start and end apart: 4 -> 4, of which waited for: 4 -> 3; matrix products, arithmetic and copies ran while one was open for 3% -> 32% of each run, Pallas kernels for 0% -> 0%
where the time goes in v1:
time: 1010 us; the launch traced here: 998 us
  waiting for transfers between devices  502 us (50%)
  local copies, waits for them, and re-layouts  332 us (33%)
  starting transfers between devices  103 us (10%)
  matrix products  50.9 us (5%)
    all_to_all x1, waiting for transfers between devices, gather_from_all(): return lax.all_to_all(copies, axis, dim, dim, tiled=True)  472 us
    unnamed x337, local copies, waits for them, and re-layouts  310 us
    all_to_all x1, starting transfers between devices, per_device(): lax.all_to_all(found, ('grp', 'fsdp'), split_axis=0, concat_axis=0, tiled...  74.9 us
  transfers between devices with their start and end apart: 4, of which 3 were waited for; matrix products, arithmetic and copies ran while one was open for 32% of the time, Pallas kernels for 0%

profile of v1, /device:TPU:1, one launch (start us, length us, event | category | flops | bytes accessed | tf_op | source)
XLA Modules:
  0.0 998.5 jit_solution(75160616515284141)
XLA Ops:
  5.0 11.5 %all-to-all-start.1 = ((s32[128,1,2]{2,1,0:T(1,128)}), s32[128,1,2]{2,1,0:T(1,128)S(1)}, u32[]{:S(2)}, u32[]{:S(2)}) async-start(s32[128,1,2]{2,1,0:T(1,128)} %bitcast.11), calls=%async_computation.1 | async-start | bytes 131072 | tf_op jit(solution)/shard_map/all_to_all | solution.py:117
  21.5 1.7 constant_dynamic-update-slice_fusion.196
  27.9 1.7 constant_dynamic-update-slice_fusion.319
  32.9 1.6 constant_dynamic-update-slice_fusion.65
  34.5 1.7 constant_dynamic-update-slice_fusion.318
  39.4 1.6 constant_dynamic-update-slice_fusion.64
  41.0 1.7 constant_dynamic-update-slice_fusion.317
  47.5 1.7 constant_dynamic-update-slice_fusion.316
  54.0 1.7 constant_dynamic-update-slice_fusion.315
  60.5 1.7 constant_dynamic-update-slice_fusion.314
  67.0 1.7 constant_dynamic-update-slice_fusion.313
  72.0 1.6 constant_dynamic-update-slice_fusion.59
  73.6 1.7 constant_dynamic-update-slice_fusion.123
  78.5 1.6 constant_dynamic-update-slice_fusion.58
  80.1 1.7 constant_dynamic-update-slice_fusion.312
  86.6 1.7 constant_dynamic-update-slice_fusion.311
  91.5 1.6 constant_dynamic-update-slice_fusion.56
  93.1 1.7 constant_dynamic-update-slice_fusion.310
  98.0 1.6 constant_dynamic-update-slice_fusion.55
  99.6 1.7 constant_dynamic-update-slice_fusion.309
  106.1 1.7 constant_dynamic-update-slice_fusion.308
  112.6 1.7 constant_dynamic-update-slice_fusion.307
  119.1 1.7 constant_dynamic-update-slice_fusion.306
  125.6 1.7 constant_dynamic-update-slice_fusion.48
  132.0 1.7 constant_dynamic-update-slice_fusion.305
  138.5 1.7 constant_dynamic-update-slice_fusion.304
  145.1 1.7 constant_dynamic-update-slice_fusion.303
  150.0 1.6 constant_dynamic-update-slice_fusion.43
  151.6 1.7 constant_dynamic-update-slice_fusion.302
  158.1 1.7 constant_dynamic-update-slice_fusion.301
  164.6 1.7 constant_dynamic-update-slice_fusion.300
  171.1 1.7 constant_dynamic-update-slice_fusion.299
  177.6 1.7 constant_dynamic-update-slice_fusion.298
  182.5 1.6 constant_dynamic-update-slice_fusion.38
  184.1 1.7 constant_dynamic-update-slice_fusion.297
  190.6 1.7 constant_dynamic-update-slice_fusion.296
  197.1 1.7 constant_dynamic-update-slice_fusion.295
  203.6 1.7 constant_dynamic-update-slice_fusion.294
  210.1 1.7 constant_dynamic-update-slice_fusion.293
  216.6 1.7 constant_dynamic-update-slice_fusion.292
  327.4 10.9 %all-to-all-start = ((bf16[64,32,6912]{2,1,0:T(8,128)(2,1)}), bf16[64,32,6912]{2,1,0:T(8,128)(2,1)}, u32[]{:S(2)}, u32[]{:S(2)}) async-start(bf16[64,32,6912]{2,1,0:T(8,128)(2,1)} %bitcast.1), calls=%async_computation | async-start | bytes 56623104 | tf_op jit(solution)/shard_map/all_to_all | solution.py:17
  339.5 471.7 %all-to-all-done = bf16[64,32,6912]{2,1,0:T(8,128)(2,1)} async-done(((bf16[64,32,6912]{2,1,0:T(8,128)(2,1)}), bf16[64,32,6912]{2,1,0:T(8,128)(2,1)}, u32[]{:S(2)}, u32[]{:S(2)}) %all-to-all-start) | async-done | bytes 28311584 | tf_op jit(solution)/shard_map/all_to_all | solution.py:17
  811.2 4.6 fusion.14
  815.7 5.2 fusion.35
  823.4 2.0 copy.51
  825.5 74.9 %all-to-all-start.2 = ((bf16[128,2,2048]{2,1,0:T(2,128)(2,1)}), bf16[128,2,2048]{2,1,0:T(2,128)(2,1)}, u32[]{:S(2)}, u32[]{:S(2)}) async-start(bf16[128,2,2048]{2,1,0:T(2,128)(2,1)} %copy.51), calls=%async_computation.2 | async-start | bytes 2097152 | tf_op jit(solution)/shard_map/all_to_all | solution.py:119
  900.3 1.6 copy.75
  903.7 14.1 %all-to-all-done.2 = bf16[128,2,2048]{2,1,0:T(2,128)(2,1)} async-done(((bf16[128,2,2048]{2,1,0:T(2,128)(2,1)}), bf16[128,2,2048]{2,1,0:T(2,128)(2,1)}, u32[]{:S(2)}, u32[]{:S(2)}) %all-to-all-start.2) | async-done | bytes 1048608 | tf_op jit(solution)/shard_map/all_to_all | solution.py:119
  919.3 1.7 gather_fusion
  921.0 8.4 fusion.8
  930.7 1.9 fusion.38
  932.6 3.3 fusion.99
  936.4 2.2 fusion.22
  938.6 3.3 fusion.40
  942.0 4.1 fusion.95
  946.1 1.8 fusion.51
  948.0 2.1 fusion.104
  950.1 2.9 copy.74
  953.0 3.4 add_convert_fusion
  956.9 3.3 fusion.28
  960.3 10.1 %fusion.2 = f32[128,2048]{1,0:T(8,128)S(1)} fusion(bf16[2048,6912]{1,0:T(8,128)(2,1)} %bitcast.2, bf16[128,4096]{1,0:T(8,128)(2,1)} %copy-done.4, bf16[128,4096]{1,0:T(8,128)(2,1)S(1)} %copy.76, bf16[1,128,4096]{2,1,0:T(8,128)(2,1)} %param.21, f32[128]{0:T(128)S(1)} %multiply_multiply_fusion, f32[4096]{0:T(1024)S(1)} %copy-done.5, f32[128]{0:T(128)S(1)} %fusion.83), kind=kOutput, calls=%fused_computation.5 | convolution fusion | flops 2152202240 | bytes 20988928 | tf_op jit(solution)/shard_map/dot_general | solution.py:126
  970.4 1.7 scatter_custom_fusion.1
  973.8 5.5 all-to-all-start.3
  980.7 16.4 %all-to-all-done.3 = bf16[128,2,2048]{2,1,0:T(2,128)(2,1)S(1)} async-done(((bf16[128,2,2048]{2,1,0:T(2,128)(2,1)}), bf16[128,2,2048]{2,1,0:T(2,128)(2,1)S(1)}, u32[]{:S(2)}, u32[]{:S(2)}) %all-to-all-start.3) | async-done | bytes 1048608 | tf_op jit(solution)/shard_map/all_to_all | solution.py:128
  (343 shorter events, 263.9 us)
Async XLA Ops:
  0.6 223.8 %copy-start.2 = (bf16[32,256]{1,0:T(8,128)(2,1)S(1)}, bf16[32,256]{1,0:T(8,128)(2,1)}, u32[]{:S(2)}) copy-start(bf16[32,256]{1,0:T(8,128)(2,1)} %param.13) | copy-start | bytes 49156
  0.6 224.4 %copy-start.3 = (bf16[32,256]{1,0:T(8,128)(2,1)S(1)}, bf16[32,256]{1,0:T(8,128)(2,1)}, u32[]{:S(2)}) copy-start(bf16[32,256]{1,0:T(8,128)(2,1)} %param.14) | copy-start | bytes 49156
  0.7 225.0 %copy-start.1 = (bf16[32,2048]{1,0:T(8,128)(2,1)S(1)}, bf16[32,2048]{1,0:T(8,128)(2,1)}, u32[]{:S(2)}) copy-start(bf16[32,2048]{1,0:T(8,128)(2,1)} %param.12) | copy-start | bytes 393220
  0.7 222.4 %copy-start = (bf16[32,4096]{1,0:T(8,128)(2,1)S(1)}, bf16[32,4096]{1,0:T(8,128)(2,1)}, u32[]{:S(2)}) copy-start(bf16[32,4096]{1,0:T(8,128)(2,1)} %param.16) | copy-start | bytes 786436
  5.0 322.4 %all-to-all-start.1 = ((s32[128,1,2]{2,1,0:T(1,128)}), s32[128,1,2]{2,1,0:T(1,128)S(1)}, u32[]{:S(2)}, u32[]{:S(2)}) async-start(s32[128,1,2]{2,1,0:T(1,128)} %bitcast.11), calls=%async_computation.1 | async-start | bytes 131072 | tf_op jit(solution)/shard_map/all_to_all | solution.py:117
  327.4 483.8 %all-to-all-start = ((bf16[64,32,6912]{2,1,0:T(8,128)(2,1)}), bf16[64,32,6912]{2,1,0:T(8,128)(2,1)}, u32[]{:S(2)}, u32[]{:S(2)}) async-start(bf16[64,32,6912]{2,1,0:T(8,128)(2,1)} %bitcast.1), calls=%async_computation | async-start | bytes 56623104 | tf_op jit(solution)/shard_map/all_to_all | solution.py:17
  338.3 484.5 %copy-start.7 = (f32[2048]{0:T(1024)S(1)}, f32[2048]{0:T(1024)}, u32[]{:S(2)}) copy-start(f32[2048]{0:T(1024)} %param.15) | copy-start | bytes 24580
  338.3 563.7 %copy-start.8 = (s32[1,128,1]{1,2,0:T(1,128)S(1)}, s32[1,128,1]{1,2,0:T(1,128)}, u32[]{:S(2)}) copy-start(s32[1,128,1]{1,2,0:T(1,128)} %param.19) | copy-start | bytes 1540
  822.9 106.5 %copy-start.6 = (bf16[4,2048]{1,0:T(4,128)(2,1)}, bf16[4,2048]{1,0:T(4,128)(2,1)S(1)}, u32[]{:S(2)}) copy-start(bf16[4,2048]{1,0:T(4,128)(2,1)S(1)} %multiply_convert_fusion) | copy-start | bytes 49156
  825.5 92.3 %all-to-all-start.2 = ((bf16[128,2,2048]{2,1,0:T(2,128)(2,1)}), bf16[128,2,2048]{2,1,0:T(2,128)(2,1)}, u32[]{:S(2)}, u32[]{:S(2)}) async-start(bf16[128,2,2048]{2,1,0:T(2,128)(2,1)} %copy.51), calls=%async_computation.2 | async-start | bytes 2097152 | tf_op jit(solution)/shard_map/all_to_all | solution.py:119
  903.3 27.1 %copy-start.5 = (f32[4096]{0:T(1024)S(1)}, f32[4096]{0:T(1024)}, u32[]{:S(2)}) copy-start(f32[4096]{0:T(1024)} %param.17) | copy-start | bytes 49156
  929.4 1.0 copy-start.4
  973.8 23.3 %all-to-all-start.3 = ((bf16[128,2,2048]{2,1,0:T(2,128)(2,1)}), bf16[128,2,2048]{2,1,0:T(2,128)(2,1)S(1)}, u32[]{:S(2)}, u32[]{:S(2)}) async-start(bf16[128,2,2048]{2,1,0:T(2,128)(2,1)} %convert_element_type.128), calls=%async_computation.3 | async-start | bytes 2097152 | tf_op jit(solution)/shard_map/all_to_all | solution.py:128
